TPU v7x, 128 devices: a whole 4x4x4 slice. The times are simulated.
128 devices in a mesh: dp: 16 (over x, z_lo, core), ctx: 8 (over z_hi, y).
Axes of the slice: x: 4, y: 4, z: 4 (z_hi: 2, z_lo: 2; z = z_hi * 2 + z_lo), core: 2. Of those that a mesh axis runs over, the one named last changes fastest.
Arguments:
- query_rows: bfloat16 [16, 2048, 2048], P('dp', 'ctx'), may hold values from -6 to 6
- key_rows: bfloat16 [16, 2048, 2048], P('dp', 'ctx'), may hold values from -6 to 6
- value_rows: bfloat16 [16, 2048, 2048], P('dp', 'ctx'), may hold values from -6 to 6
- utt_lengths: int32 [16, 8], P('dp'), may hold values from 1 to 1024, 2048 in all within a row
- out_weight: bfloat16 [2048, 4096], P('dp'), may hold values from -0.5 to 0.5
Outputs:
- out_rows: bfloat16 [16, 2048, 4096], P('dp', 'ctx')
Inputs may be any that keep to these rules, and one draw needn't show every extreme that they name: `utt_lengths`: the 8 lengths of each sequence sum to 2048, and in each sequence one utterance has exactly 1024 frames.
All inputs are finite; a program needn't handle non-finite values.
Results may differ from a plain program's by a relative error of at most 0.015.
Values may be sent and summed in bfloat16 or wider, within the bound.
No kernel may reach another device: no remote copies, remote signals or barrier semaphores. Data moves between devices by JAX's collectives and lax.ppermute only.
A program may use at most 192 MiB of HBM per device.

v0:
```python
import jax
import jax.numpy as jnp
from jax import lax
from jax.sharding import PartitionSpec as P

HQ = 16
HD = 128


big_negative = -1e30


def from_behind(block, axis, distance):
    devices = range(lax.axis_size(axis))
    route = [((i - distance) % len(devices), i) for i in devices]
    return lax.ppermute(block, axis, route)


def segment_ids(utt_ends, first_frame, frames):
    positions = first_frame + jnp.arange(frames, dtype=jnp.int32)
    return jnp.sum((positions[:, None] >= utt_ends[None, :]).astype(jnp.int32), axis=1)


def attend(carry_state, query_heads, query_seg, kv_block, key_seg):
    max_old, denom_old, numerator = carry_state
    frames = kv_block.shape[1]
    key_heads = kv_block[0].reshape(frames, HQ, HD)
    value_heads = kv_block[1].reshape(frames, HQ, HD)
    allowed = (query_seg[:, None] == key_seg[None, :])[:, None, :]
    scores = jnp.einsum(
        "qhd,khd->qhk", query_heads, key_heads, preferred_element_type=jnp.float32
    ) * HD ** (-0.5)
    masked = jnp.where(allowed, scores, big_negative)
    max_new = jnp.maximum(max_old, jnp.max(masked, axis=2))
    weights = jnp.where(allowed, jnp.exp(masked - max_new[:, :, None]), 0.0)
    rescale = jnp.exp(max_old - max_new)
    denom_new = denom_old * rescale + jnp.sum(weights, axis=2)
    numerator = numerator * rescale[:, :, None] + jnp.einsum(
        "qhk,khd->qhd",
        weights.astype(jnp.bfloat16),
        value_heads,
        preferred_element_type=jnp.float32,
    )
    return (max_new, denom_new, numerator)


def shards(query_rows, key_rows, value_rows, utt_lengths, out_weight):
    frames = query_rows.shape[1]
    cycle_size = lax.axis_size("ctx")
    cycle_place = lax.axis_index("ctx")
    utt_ends = jnp.cumsum(utt_lengths[0])
    query_heads = query_rows[0].reshape(frames, HQ, HD)
    query_seg = segment_ids(utt_ends, cycle_place * frames, frames)

    def absorb(carry_state, kv_block, source):
        key_seg = segment_ids(utt_ends, source * frames, frames)
        return attend(carry_state, query_heads, query_seg, kv_block, key_seg)

    initial = (
        jnp.full((frames, HQ), big_negative, jnp.float32),
        jnp.zeros((frames, HQ), jnp.float32),
        jnp.zeros((frames, HQ, HD), jnp.float32),
    )
    kv_block = jnp.concatenate([key_rows, value_rows], axis=0)
    carry_state = absorb(initial, kv_block, cycle_place)
    travelling = kv_block
    for hop_index in range(1, cycle_size):
        travelling = from_behind(travelling, "ctx", 1)
        carry_state = absorb(carry_state, travelling, (cycle_place - hop_index) % cycle_size)
    max_final, denom_final, numerator = carry_state
    attn_rows = (numerator / denom_final[:, :, None]).reshape(frames, HQ * HD).astype(jnp.bfloat16)
    summed = jnp.dot(
        attn_rows,
        lax.all_gather(out_weight, "dp", axis=0, tiled=True),
        preferred_element_type=jnp.float32,
    )
    return summed.astype(jnp.bfloat16)[None]


def solution(mesh):
    return jax.shard_map(
        shards,
        mesh=mesh,
        in_specs=(
            P("dp", "ctx", None),
            P("dp", "ctx", None),
            P("dp", "ctx", None),
            P("dp", None),
            P("dp", None),
        ),
        out_specs=P("dp", "ctx", None),
        check_vma=False,
    )
```

profile of v0, /device:TPU:102, one launch (start us, length us, event | category | flops | bytes accessed | tf_op | source)
XLA Modules:
  0.0 427.6 jit_solution(228833962925564834)
XLA Ops:
  7.3 1.5 copy.100
  8.8 1.6 copy.62
  10.5 1.6 collective-permute-start
  12.2 49.5 %collective-permute-done = bf16[2,256,2048]{1,2,0:T(8,128)(2,1)S(1)} collective-permute-done((bf16[2,256,2048]{1,2,0:T(8,128)(2,1)S(1)}, bf16[2,256,2048]{1,2,0:T(8,128)(2,1)S(1)}, u32[]{:S(2)}, u32[]{:S(2)}) %collective-permute-start) | collective-permute-done | bytes 2097184 | tf_op jit(solution)/shard_map/ppermute | solution.py:16
  61.7 50.2 %collective-permute-done.1 = bf16[2,256,2048]{1,2,0:T(8,128)(2,1)S(1)} collective-permute-done((bf16[2,256,2048]{1,2,0:T(8,128)(2,1)S(1)}, bf16[2,256,2048]{1,2,0:T(8,128)(2,1)S(1)}, u32[]{:S(2)}, u32[]{:S(2)}) %collective-permute-start.1) | collective-permute-done | bytes 2097184 | tf_op jit(solution)/shard_map/ppermute | solution.py:16
  111.9 1.3 copy-done.1
  113.2 49.4 %collective-permute-done.2 = bf16[2,256,2048]{1,2,0:T(8,128)(2,1)} collective-permute-done((bf16[2,256,2048]{1,2,0:T(8,128)(2,1)S(1)}, bf16[2,256,2048]{1,2,0:T(8,128)(2,1)}, u32[]{:S(2)}, u32[]{:S(2)}) %collective-permute-start.2) | collective-permute-done | bytes 2097184 | tf_op jit(solution)/shard_map/ppermute | solution.py:16
  162.7 1.4 copy.102
  164.5 46.8 %collective-permute-done.3 = bf16[2,256,2048]{1,2,0:T(8,128)(2,1)} collective-permute-done((bf16[2,256,2048]{1,2,0:T(8,128)(2,1)}, bf16[2,256,2048]{1,2,0:T(8,128)(2,1)}, u32[]{:S(2)}, u32[]{:S(2)}) %collective-permute-start.3) | collective-permute-done | bytes 2097184 | tf_op jit(solution)/shard_map/ppermute | solution.py:16
  213.2 1.0 fusion.2
  214.2 44.8 %collective-permute-done.4 = bf16[2,256,2048]{1,2,0:T(8,128)(2,1)S(1)} collective-permute-done((bf16[2,256,2048]{1,2,0:T(8,128)(2,1)}, bf16[2,256,2048]{1,2,0:T(8,128)(2,1)S(1)}, u32[]{:S(2)}, u32[]{:S(2)}) %collective-permute-start.4) | collective-permute-done | bytes 2097184 | tf_op jit(solution)/shard_map/ppermute | solution.py:16
  260.2 1.7 fusion.139
  261.9 1.0 fusion.4
  262.9 1.7 fusion.140
  264.6 41.0 %collective-permute-done.5 = bf16[2,256,2048]{1,2,0:T(8,128)(2,1)S(1)} collective-permute-done((bf16[2,256,2048]{1,2,0:T(8,128)(2,1)S(1)}, bf16[2,256,2048]{1,2,0:T(8,128)(2,1)S(1)}, u32[]{:S(2)}, u32[]{:S(2)}) %collective-permute-start.5) | collective-permute-done | bytes 2097184 | tf_op jit(solution)/shard_map/ppermute | solution.py:16
  305.6 1.0 fusion.5
  306.8 1.0 fusion.6
  307.9 1.1 fusion.142
  309.0 1.0 fusion.7
  310.0 41.4 %collective-permute-done.6 = bf16[2,256,2048]{1,2,0:T(8,128)(2,1)S(1)} collective-permute-done((bf16[2,256,2048]{1,2,0:T(8,128)(2,1)S(1)}, bf16[2,256,2048]{1,2,0:T(8,128)(2,1)S(1)}, u32[]{:S(2)}, u32[]{:S(2)}) %collective-permute-start.6) | collective-permute-done | bytes 2097184 | tf_op jit(solution)/shard_map/ppermute | solution.py:16
  351.4 1.2 fusion.136
  359.9 1.2 fusion.21
  362.3 1.2 fusion.39
  363.4 2.5 fusion.37
  366.0 2.5 fusion.35
  368.5 2.5 fusion.33
  371.0 2.5 fusion.31
  373.5 2.5 fusion.29
  376.1 1.2 fusion.27
  379.4 3.9 fusion.42
  383.3 25.9 %all-gather.2.cloned.1.call-done = bf16[2048,4096]{1,0:T(8,128)(2,1)} async-done(((bf16[128,4096]{1,0:T(8,128)(2,1)}), bf16[2048,4096]{1,0:T(8,128)(2,1)}) %all-gather.2.cloned.1.call-update) | async-done | bytes 16777232 | tf_op jit(solution)/shard_map/all_gather | solution.py:74
  409.2 11.5 %fusion = bf16[1,256,4096]{2,1,0:T(8,128)(2,1)} fusion(bf16[256,2048]{0,1:T(8,128)(2,1)S(1)} %bitcast.198, bf16[2048,4096]{1,0:T(8,128)(2,1)} %all-gather.2.cloned.1.call-done), kind=kOutput, calls=%fused_computation.1 | convolution fusion | flops 4296015872 | bytes 19922944 | tf_op jit(solution)/shard_map/dot_general | solution.py:72
  (75 shorter events, 14.9 us)
Async XLA Ops:
  6.5 402.7 %all-gather.2.cloned.1.call-start = ((), (), s32[]{:S(2)}) async-start(), calls=%async_computation | async-start | bytes 17825792 | tf_op jit(solution)/shard_map/all_gather | solution.py:74
  7.3 155.3 %copy-start.17 = (s32[1,8]{1,0:T(1,128)S(1)}, s32[1,8]{1,0:T(1,128)}, u32[]{:S(2)}) copy-start(s32[1,8]{1,0:T(1,128)} %param.8) | copy-start | bytes 100
  8.8 155.4 %copy-start = (bf16[1,256,2048]{2,1,0:T(8,128)(2,1)S(1)}, bf16[1,256,2048]{2,1,0:T(8,128)(2,1)}, u32[]{:S(2)}) copy-start(bf16[1,256,2048]{2,1,0:T(8,128)(2,1)} %param.6) | copy-start | bytes 3145732
  10.5 51.2 %collective-permute-start = (bf16[2,256,2048]{1,2,0:T(8,128)(2,1)S(1)}, bf16[2,256,2048]{1,2,0:T(8,128)(2,1)S(1)}, u32[]{:S(2)}, u32[]{:S(2)}) collective-permute-start(bf16[2,256,2048]{1,2,0:T(8,128)(2,1)S(1)} %pad_maximum_fusion), channel_id=1, source_target_pairs={{7,0},{0,1},{1,2},{2,3},{3,4},{4,5},{5,6},{6,7},{15,8},{8,9},{9,10... | collective-permute-start | bytes 6291464 | tf_op jit(solution)/shard_map/ppermute | solution.py:16
  61.7 100.9 %copy-start.3 = (bf16[2,256,2048]{1,2,0:T(8,128)(2,1)}, bf16[2,256,2048]{1,2,0:T(8,128)(2,1)S(1)}, u32[]{:S(2)}) copy-start(bf16[2,256,2048]{1,2,0:T(8,128)(2,1)S(1)} %collective-permute-done) | copy-start | bytes 6291460
  61.7 50.2 %collective-permute-start.1 = (bf16[2,256,2048]{1,2,0:T(8,128)(2,1)S(1)}, bf16[2,256,2048]{1,2,0:T(8,128)(2,1)S(1)}, u32[]{:S(2)}, u32[]{:S(2)}) collective-permute-start(bf16[2,256,2048]{1,2,0:T(8,128)(2,1)S(1)} %collective-permute-done), channel_id=1, source_target_pairs={{7,0},{0,1},{1,2},{2,3},{3,4},{4,5},{5,6},{6,7},{15,8},{8,9},{9,10... | collective-permute-start | bytes 6291464 | tf_op jit(solution)/shard_map/ppermute | solution.py:16
  111.9 1.3 copy-start.1
  113.2 49.4 %collective-permute-start.2 = (bf16[2,256,2048]{1,2,0:T(8,128)(2,1)S(1)}, bf16[2,256,2048]{1,2,0:T(8,128)(2,1)}, u32[]{:S(2)}, u32[]{:S(2)}) collective-permute-start(bf16[2,256,2048]{1,2,0:T(8,128)(2,1)S(1)} %collective-permute-done.1), channel_id=1, source_target_pairs={{7,0},{0,1},{1,2},{2,3},{3,4},{4,5},{5,6},{6,7},{15,8},{8,9},{9,10... | collective-permute-start | bytes 6291464 | tf_op jit(solution)/shard_map/ppermute | solution.py:16
  162.6 48.7 %collective-permute-start.3 = (bf16[2,256,2048]{1,2,0:T(8,128)(2,1)}, bf16[2,256,2048]{1,2,0:T(8,128)(2,1)}, u32[]{:S(2)}, u32[]{:S(2)}) collective-permute-start(bf16[2,256,2048]{1,2,0:T(8,128)(2,1)} %collective-permute-done.2), channel_id=1, source_target_pairs={{7,0},{0,1},{1,2},{2,3},{3,4},{4,5},{5,6},{6,7},{15,8},{8,9},{9,10... | collective-permute-start | bytes 6291464 | tf_op jit(solution)/shard_map/ppermute | solution.py:16
  164.4 48.5 %copy-start.4 = (bf16[2,256,2048]{1,2,0:T(8,128)(2,1)S(1)}, bf16[2,256,2048]{1,2,0:T(8,128)(2,1)}, u32[]{:S(2)}) copy-start(bf16[2,256,2048]{1,2,0:T(8,128)(2,1)} %copy-done.3) | copy-start | bytes 6291460
  211.3 47.7 %collective-permute-start.4 = (bf16[2,256,2048]{1,2,0:T(8,128)(2,1)}, bf16[2,256,2048]{1,2,0:T(8,128)(2,1)S(1)}, u32[]{:S(2)}, u32[]{:S(2)}) collective-permute-start(bf16[2,256,2048]{1,2,0:T(8,128)(2,1)} %collective-permute-done.3), channel_id=1, source_target_pairs={{7,0},{0,1},{1,2},{2,3},{3,4},{4,5},{5,6},{6,7},{15,8},{8,9},{9,10... | collective-permute-start | bytes 6291464 | tf_op jit(solution)/shard_map/ppermute | solution.py:16
  211.9 1.2 copy-start.15
  211.9 1.3 copy-start.13
  211.9 47.2 %copy-start.11 = (pred[256,256]{0,1:T(8,128)(4,1)}, pred[256,256]{0,1:T(8,128)(4,1)S(1)}, u32[]{:S(2)}) copy-start(pred[256,256]{0,1:T(8,128)(4,1)S(1)} %get-tuple-element.45) | copy-start | bytes 196612
  211.9 50.0 %copy-start.9 = (pred[256,256]{0,1:T(8,128)(4,1)}, pred[256,256]{0,1:T(8,128)(4,1)S(1)}, u32[]{:S(2)}) copy-start(pred[256,256]{0,1:T(8,128)(4,1)S(1)} %get-tuple-element.46) | copy-start | bytes 196612
  211.9 93.7 %copy-start.7 = (pred[256,256]{0,1:T(8,128)(4,1)}, pred[256,256]{0,1:T(8,128)(4,1)S(1)}, u32[]{:S(2)}) copy-start(pred[256,256]{0,1:T(8,128)(4,1)S(1)} %get-tuple-element.47) | copy-start | bytes 196612
  213.1 45.9 %copy-start.2 = (bf16[2,256,2048]{1,2,0:T(8,128)(2,1)S(1)}, bf16[2,256,2048]{1,2,0:T(8,128)(2,1)}, u32[]{:S(2)}) copy-start(bf16[2,256,2048]{1,2,0:T(8,128)(2,1)} %copy-done.1) | copy-start | bytes 6291460
  259.0 46.6 %collective-permute-start.5 = (bf16[2,256,2048]{1,2,0:T(8,128)(2,1)S(1)}, bf16[2,256,2048]{1,2,0:T(8,128)(2,1)S(1)}, u32[]{:S(2)}, u32[]{:S(2)}) collective-permute-start(bf16[2,256,2048]{1,2,0:T(8,128)(2,1)S(1)} %collective-permute-done.4), channel_id=1, source_target_pairs={{7,0},{0,1},{1,2},{2,3},{3,4},{4,5},{5,6},{6,7},{15,8},{8,9},{9,10... | collective-permute-start | bytes 6291464 | tf_op jit(solution)/shard_map/ppermute | solution.py:16
  305.6 45.8 %collective-permute-start.6 = (bf16[2,256,2048]{1,2,0:T(8,128)(2,1)S(1)}, bf16[2,256,2048]{1,2,0:T(8,128)(2,1)S(1)}, u32[]{:S(2)}, u32[]{:S(2)}) collective-permute-start(bf16[2,256,2048]{1,2,0:T(8,128)(2,1)S(1)} %collective-permute-done.5), channel_id=1, source_target_pairs={{7,0},{0,1},{1,2},{2,3},{3,4},{4,5},{5,6},{6,7},{15,8},{8,9},{9,10... | collective-permute-start | bytes 6291464 | tf_op jit(solution)/shard_map/ppermute | solution.py:16
  352.6 1.1 copy-start.16
  352.6 2.1 copy-start.14
  353.7 2.1 copy-start.12
  354.7 2.1 copy-start.10
  355.8 2.1 copy-start.8
  373.5 2.5 copy-start.5
  373.5 3.7 copy-start.21
  376.1 1.2 copy-start.6
  376.1 2.0 copy-start.18
  376.1 2.7 copy-start.19
  376.1 3.4 copy-start.20
Sparse Core Ops, SparseCore 0:
  9.0 400.1 all-gather.1
where the time goes:
time: 433 us; the launch traced here: 428 us
  waiting for transfers between devices  350 us (81%)
  matrix products  38.6 us (9%)
  local copies, waits for them, and re-layouts  14.3 us (3%)
  between operations  13.9 us (3%)
  other arithmetic  9.43 us (2%)
    ppermute x7, waiting for transfers between devices, from_behind(): return lax.ppermute(block, axis, route)  323 us
    all_gather x1, waiting for transfers between devices, shards(): lax.all_gather(out_weight, 'dp', axis=0, tiled=True)  25.9 us
    dot_general x8, matrix products, attend(): jnp.einsum('qhk,khd->qhd', weights.astype(jnp.bfloat16), value_heads, pre...  18.9 us
    dot_general x1, matrix products, shards(): jnp.dot(attn_rows, lax.all_gather(out_weight, 'dp', axis=0, tiled=True),...  11.5 us
  transfers between devices with their start and end apart: 8, of which 8 were waited for; matrix products, arithmetic and copies ran while one was open for 11% of the time, Pallas kernels for 0%

commit v1 on v0

--- a/solution.py
+++ b/solution.py
@@ -61,17 +61,23 @@
         jnp.zeros((frames, HQ), jnp.float32),
         jnp.zeros((frames, HQ, HD), jnp.float32),
     )
+    gathered_weight = lax.all_gather(out_weight, "dp", axis=0, tiled=True)
     kv_block = jnp.concatenate([key_rows, value_rows], axis=0)
     carry_state = absorb(initial, kv_block, cycle_place)
-    travelling = kv_block
-    for hop_index in range(1, cycle_size):
-        travelling = from_behind(travelling, "ctx", 1)
-        carry_state = absorb(carry_state, travelling, (cycle_place - hop_index) % cycle_size)
+    ahead = kv_block
+    behind = kv_block
+    for hop_index in range(1, cycle_size // 2 + 1):
+        ahead = from_behind(ahead, "ctx", 1)
+        if hop_index < cycle_size - cycle_size // 2:
+            behind = from_behind(behind, "ctx", -1)
+        carry_state = absorb(carry_state, ahead, (cycle_place - hop_index) % cycle_size)
+        if hop_index < cycle_size - cycle_size // 2:
+            carry_state = absorb(carry_state, behind, (cycle_place + hop_index) % cycle_size)
     max_final, denom_final, numerator = carry_state
     attn_rows = (numerator / denom_final[:, :, None]).reshape(frames, HQ * HD).astype(jnp.bfloat16)
     summed = jnp.dot(
         attn_rows,
-        lax.all_gather(out_weight, "dp", axis=0, tiled=True),
+        gathered_weight,
         preferred_element_type=jnp.float32,
     )
     return summed.astype(jnp.bfloat16)[None]

time: 433 us -> 300 us (0.69)
  waiting for transfers between devices: 350 us -> 204 us
  starting transfers between devices: 1.66 us -> 17.1 us
    ppermute x7, waiting for transfers between devices: 323 us -> 169 us  [from_behind(): return lax.ppermute(block, axis, route)]
    ppermute x7, starting transfers between devices: 1.66 us -> 17.1 us  [from_behind(): return lax.ppermute(block, axis, route)]
    all_gather x1, waiting for transfers between devices: 25.9 us -> 35.2 us  [shards(): gathered_weight = lax.all_gather(out_weight, 'dp', axis=0, tiled=True)]
  transfers between devices with their start and end apart: 8 -> 8, of which waited for: 8 -> 5; matrix products, arithmetic and copies ran while one was open for 11% -> 15% of each run, Pallas kernels for 0% -> 0%
where the time goes in v1:
time: 300 us; the launch traced here: 294 us
  waiting for transfers between devices  204 us (68%)
  matrix products  35.9 us (12%)
  starting transfers between devices  17.1 us (6%)
  between operations  13.9 us (5%)
  other arithmetic  11.6 us (4%)
  local copies, waits for them, and re-layouts  11.2 us (4%)
    ppermute x7, waiting for transfers between devices, from_behind(): return lax.ppermute(block, axis, route)  169 us
    all_gather x1, waiting for transfers between devices, shards(): gathered_weight = lax.all_gather(out_weight, 'dp', axis=0, tiled=True)  35.2 us
    ppermute x7, starting transfers between devices, from_behind(): return lax.ppermute(block, axis, route)  17.1 us
    dot_general x8, matrix products, attend(): jnp.einsum('qhk,khd->qhd', weights.astype(jnp.bfloat16), value_heads, pre...  16.2 us
    dot_general x1, matrix products, shards(): jnp.dot(attn_rows, gathered_weight, preferred_element_type=jnp.float32)  11.5 us
    reduce_sum x8, other arithmetic, attend(): denom_new = denom_old * rescale + jnp.sum(weights, axis=2)  9.25 us
    dot_general x8, matrix products, attend(): jnp.einsum('qhd,khd->qhk', query_heads, key_heads, preferred_element_type...  8.26 us
  transfers between devices with their start and end apart: 8, of which 5 were waited for; matrix products, arithmetic and copies ran while one was open for 15% of the time, Pallas kernels for 0%

profile of v1, /device:TPU:102, one launch (start us, length us, event | category | flops | bytes accessed | tf_op | source)
XLA Modules:
  0.0 294.2 jit_solution(9409193112712245634)
XLA Ops:
  7.3 1.5 copy.100
  8.8 1.6 copy.62
  10.3 1.5 pad_maximum_fusion
  11.8 1.6 collective-permute-start
  13.4 4.1 %collective-permute-start.1 = (bf16[2,256,2048]{1,2,0:T(8,128)(2,1)}, bf16[2,256,2048]{1,2,0:T(8,128)(2,1)}, u32[]{:S(2)}, u32[]{:S(2)}) collective-permute-start(bf16[2,256,2048]{1,2,0:T(8,128)(2,1)} %pad_maximum_fusion), channel_id=1, source_target_pairs={{1,0},{2,1},{3,2},{4,3},{5,4},{6,5},{7,6},{0,7},{9,8},{10,9},{11,1... | collective-permute-start | bytes 6291464 | tf_op jit(solution)/shard_map/ppermute | solution.py:16
  17.7 1.4 copy.102
  19.4 43.9 %collective-permute-done = bf16[2,256,2048]{1,2,0:T(8,128)(2,1)} collective-permute-done((bf16[2,256,2048]{1,2,0:T(8,128)(2,1)}, bf16[2,256,2048]{1,2,0:T(8,128)(2,1)}, u32[]{:S(2)}, u32[]{:S(2)}) %collective-permute-start) | collective-permute-done | bytes 2097184 | tf_op jit(solution)/shard_map/ppermute | solution.py:16
  63.9 5.7 %collective-permute-start.3 = (bf16[2,256,2048]{1,2,0:T(8,128)(2,1)}, bf16[2,256,2048]{1,2,0:T(8,128)(2,1)S(1)}, u32[]{:S(2)}, u32[]{:S(2)}) collective-permute-start(bf16[2,256,2048]{1,2,0:T(8,128)(2,1)} %collective-permute-done.1), channel_id=1, source_target_pairs={{1,0},{2,1},{3,2},{4,3},{5,4},{6,5},{7,6},{0,7},{9,8},{10,9},{11,1... | collective-permute-start | bytes 6291464 | tf_op jit(solution)/shard_map/ppermute | solution.py:16
  70.6 1.7 fusion.138
  72.3 1.7 fusion.137
  74.0 39.6 %collective-permute-done.2 = bf16[2,256,2048]{1,2,0:T(8,128)(2,1)S(1)} collective-permute-done((bf16[2,256,2048]{1,2,0:T(8,128)(2,1)}, bf16[2,256,2048]{1,2,0:T(8,128)(2,1)S(1)}, u32[]{:S(2)}, u32[]{:S(2)}) %collective-permute-start.2) | collective-permute-done | bytes 2097184 | tf_op jit(solution)/shard_map/ppermute | solution.py:16
  114.7 1.0 fusion.2
  115.7 5.7 %collective-permute-start.5 = (bf16[2,256,2048]{1,2,0:T(8,128)(2,1)S(1)}, bf16[2,256,2048]{1,2,0:T(8,128)(2,1)S(1)}, u32[]{:S(2)}, u32[]{:S(2)}) collective-permute-start(bf16[2,256,2048]{1,2,0:T(8,128)(2,1)S(1)} %collective-permute-done.3), channel_id=1, source_target_pairs={{1,0},{2,1},{3,2},{4,3},{5,4},{6,5},{7,6},{0,7},{9,8},{10,9},{11,1... | collective-permute-start | bytes 6291464 | tf_op jit(solution)/shard_map/ppermute | solution.py:16
  121.6 1.0 fusion.5
  122.8 40.1 %collective-permute-done.4 = bf16[2,256,2048]{1,2,0:T(8,128)(2,1)S(1)} collective-permute-done((bf16[2,256,2048]{1,2,0:T(8,128)(2,1)S(1)}, bf16[2,256,2048]{1,2,0:T(8,128)(2,1)S(1)}, u32[]{:S(2)}, u32[]{:S(2)}) %collective-permute-start.4) | collective-permute-done | bytes 2097184 | tf_op jit(solution)/shard_map/ppermute | solution.py:16
  162.9 1.0 fusion.4
  164.1 1.0 fusion.6
  165.3 1.0 fusion.7
  166.3 45.0 %collective-permute-done.6 = bf16[2,256,2048]{1,2,0:T(8,128)(2,1)S(1)} collective-permute-done((bf16[2,256,2048]{1,2,0:T(8,128)(2,1)S(1)}, bf16[2,256,2048]{1,2,0:T(8,128)(2,1)S(1)}, u32[]{:S(2)}, u32[]{:S(2)}) %collective-permute-start.6) | collective-permute-done | bytes 2097184 | tf_op jit(solution)/shard_map/ppermute | solution.py:16
  211.4 1.0 fusion.8
  212.5 1.9 fusion.9
  219.6 1.2 fusion.21
  221.9 2.5 fusion.39
  224.5 2.5 fusion.37
  227.0 2.5 fusion.35
  229.5 2.5 fusion.33
  232.0 1.2 fusion.31
  233.2 1.2 fusion.29
  234.4 1.2 fusion.27
  238.0 2.6 fusion.42
  240.6 35.2 %all-gather.2.cloned.1.call-done = bf16[2048,4096]{1,0:T(8,128)(2,1)} async-done(((bf16[128,4096]{1,0:T(8,128)(2,1)}), bf16[2048,4096]{1,0:T(8,128)(2,1)}) %all-gather.2.cloned.1.call-update) | async-done | bytes 16777232 | tf_op jit(solution)/shard_map/all_gather | solution.py:64
  275.9 11.5 %fusion = bf16[1,256,4096]{2,1,0:T(8,128)(2,1)} fusion(bf16[256,2048]{0,1:T(8,128)(2,1)S(1)} %bitcast.198, bf16[2048,4096]{1,0:T(8,128)(2,1)} %all-gather.2.cloned.1.call-done), kind=kOutput, calls=%fused_computation.1 | convolution fusion | flops 4296015872 | bytes 19922944 | tf_op jit(solution)/shard_map/dot_general | solution.py:78
  (63 shorter events, 13.2 us)
Async XLA Ops:
  6.5 269.3 %all-gather.2.cloned.1.call-start = ((), (), s32[]{:S(2)}) async-start(), calls=%async_computation | async-start | bytes 17825792 | tf_op jit(solution)/shard_map/all_gather | solution.py:64
  7.3 10.2 %copy-start.11 = (s32[1,8]{1,0:T(1,128)S(1)}, s32[1,8]{1,0:T(1,128)}, u32[]{:S(2)}) copy-start(s32[1,8]{1,0:T(1,128)} %param.8) | copy-start | bytes 100
  8.8 10.4 %copy-start = (bf16[1,256,2048]{2,1,0:T(8,128)(2,1)S(1)}, bf16[1,256,2048]{2,1,0:T(8,128)(2,1)}, u32[]{:S(2)}) copy-start(bf16[1,256,2048]{2,1,0:T(8,128)(2,1)} %param.6) | copy-start | bytes 3145732
  11.8 51.4 %collective-permute-start = (bf16[2,256,2048]{1,2,0:T(8,128)(2,1)}, bf16[2,256,2048]{1,2,0:T(8,128)(2,1)}, u32[]{:S(2)}, u32[]{:S(2)}) collective-permute-start(bf16[2,256,2048]{1,2,0:T(8,128)(2,1)} %pad_maximum_fusion), channel_id=1, source_target_pairs={{7,0},{0,1},{1,2},{2,3},{3,4},{4,5},{5,6},{6,7},{15,8},{8,9},{9,10... | collective-permute-start | bytes 6291464 | tf_op jit(solution)/shard_map/ppermute | solution.py:16
  13.4 50.5 %collective-permute-start.1 = (bf16[2,256,2048]{1,2,0:T(8,128)(2,1)}, bf16[2,256,2048]{1,2,0:T(8,128)(2,1)}, u32[]{:S(2)}, u32[]{:S(2)}) collective-permute-start(bf16[2,256,2048]{1,2,0:T(8,128)(2,1)} %pad_maximum_fusion), channel_id=1, source_target_pairs={{1,0},{2,1},{3,2},{4,3},{5,4},{6,5},{7,6},{0,7},{9,8},{10,9},{11,1... | collective-permute-start | bytes 6291464 | tf_op jit(solution)/shard_map/ppermute | solution.py:16
  63.2 50.4 %collective-permute-start.2 = (bf16[2,256,2048]{1,2,0:T(8,128)(2,1)}, bf16[2,256,2048]{1,2,0:T(8,128)(2,1)S(1)}, u32[]{:S(2)}, u32[]{:S(2)}) collective-permute-start(bf16[2,256,2048]{1,2,0:T(8,128)(2,1)} %collective-permute-done), channel_id=1, source_target_pairs={{7,0},{0,1},{1,2},{2,3},{3,4},{4,5},{5,6},{6,7},{15,8},{8,9},{9,10... | collective-permute-start | bytes 6291464 | tf_op jit(solution)/shard_map/ppermute | solution.py:16
  63.9 49.8 %copy-start.5 = (pred[256,256]{0,1:T(8,128)(4,1)}, pred[256,256]{0,1:T(8,128)(4,1)S(1)}, u32[]{:S(2)}) copy-start(pred[256,256]{0,1:T(8,128)(4,1)S(1)} %get-tuple-element.45) | copy-start | bytes 196612
  63.9 50.8 %copy-start.7 = (pred[256,256]{0,1:T(8,128)(4,1)}, pred[256,256]{0,1:T(8,128)(4,1)S(1)}, u32[]{:S(2)}) copy-start(pred[256,256]{0,1:T(8,128)(4,1)S(1)} %get-tuple-element.51) | copy-start | bytes 196612
  63.9 51.8 %copy-start.9 = (pred[256,256]{0,1:T(8,128)(4,1)}, pred[256,256]{0,1:T(8,128)(4,1)S(1)}, u32[]{:S(2)}) copy-start(pred[256,256]{0,1:T(8,128)(4,1)S(1)} %get-tuple-element.44) | copy-start | bytes 196612
  63.9 57.7 %copy-start.1 = (pred[256,256]{0,1:T(8,128)(4,1)}, pred[256,256]{0,1:T(8,128)(4,1)S(1)}, u32[]{:S(2)}) copy-start(pred[256,256]{0,1:T(8,128)(4,1)S(1)} %get-tuple-element.47) | copy-start | bytes 196612
  63.9 99.0 %copy-start.3 = (pred[256,256]{0,1:T(8,128)(4,1)}, pred[256,256]{0,1:T(8,128)(4,1)S(1)}, u32[]{:S(2)}) copy-start(pred[256,256]{0,1:T(8,128)(4,1)S(1)} %get-tuple-element.46) | copy-start | bytes 196612
  63.9 51.8 %collective-permute-start.3 = (bf16[2,256,2048]{1,2,0:T(8,128)(2,1)}, bf16[2,256,2048]{1,2,0:T(8,128)(2,1)S(1)}, u32[]{:S(2)}, u32[]{:S(2)}) collective-permute-start(bf16[2,256,2048]{1,2,0:T(8,128)(2,1)} %collective-permute-done.1), channel_id=1, source_target_pairs={{1,0},{2,1},{3,2},{4,3},{5,4},{6,5},{7,6},{0,7},{9,8},{10,9},{11,1... | collective-permute-start | bytes 6291464 | tf_op jit(solution)/shard_map/ppermute | solution.py:16
  113.6 49.3 %collective-permute-start.4 = (bf16[2,256,2048]{1,2,0:T(8,128)(2,1)S(1)}, bf16[2,256,2048]{1,2,0:T(8,128)(2,1)S(1)}, u32[]{:S(2)}, u32[]{:S(2)}) collective-permute-start(bf16[2,256,2048]{1,2,0:T(8,128)(2,1)S(1)} %collective-permute-done.2), channel_id=1, source_target_pairs={{7,0},{0,1},{1,2},{2,3},{3,4},{4,5},{5,6},{6,7},{15,8},{8,9},{9,10... | collective-permute-start | bytes 6291464 | tf_op jit(solution)/shard_map/ppermute | solution.py:16
  115.7 49.4 %collective-permute-start.5 = (bf16[2,256,2048]{1,2,0:T(8,128)(2,1)S(1)}, bf16[2,256,2048]{1,2,0:T(8,128)(2,1)S(1)}, u32[]{:S(2)}, u32[]{:S(2)}) collective-permute-start(bf16[2,256,2048]{1,2,0:T(8,128)(2,1)S(1)} %collective-permute-done.3), channel_id=1, source_target_pairs={{1,0},{2,1},{3,2},{4,3},{5,4},{6,5},{7,6},{0,7},{9,8},{10,9},{11,1... | collective-permute-start | bytes 6291464 | tf_op jit(solution)/shard_map/ppermute | solution.py:16
  162.9 48.4 %collective-permute-start.6 = (bf16[2,256,2048]{1,2,0:T(8,128)(2,1)S(1)}, bf16[2,256,2048]{1,2,0:T(8,128)(2,1)S(1)}, u32[]{:S(2)}, u32[]{:S(2)}) collective-permute-start(bf16[2,256,2048]{1,2,0:T(8,128)(2,1)S(1)} %collective-permute-done.4), channel_id=1, source_target_pairs={{7,0},{0,1},{1,2},{2,3},{3,4},{4,5},{5,6},{6,7},{15,8},{8,9},{9,10... | collective-permute-start | bytes 6291464 | tf_op jit(solution)/shard_map/ppermute | solution.py:16
  212.5 1.9 copy-start.8
  212.5 2.9 %copy-start.6 = (pred[256,256]{0,1:T(8,128)(4,1)S(1)}, pred[256,256]{0,1:T(8,128)(4,1)}, u32[]{:S(2)}) copy-start(pred[256,256]{0,1:T(8,128)(4,1)} %copy-done.5) | copy-start | bytes 196612
  214.4 2.1 copy-start.4
  215.4 2.1 copy-start.2
  219.6 2.3 copy-start.10
  234.4 1.6 copy-start.12
  234.4 2.3 copy-start.13
  234.4 3.0 %copy-start.14 = (f32[16,128,256]{2,1,0:T(8,128)S(1)}, f32[16,128,256]{2,1,0:T(8,128)}, u32[]{:S(2)}) copy-start(f32[16,128,256]{2,1,0:T(8,128)} %fusion.35) | copy-start | bytes 6291460
  234.4 3.6 %copy-start.15 = (f32[16,128,256]{2,1,0:T(8,128)S(1)}, f32[16,128,256]{2,1,0:T(8,128)}, u32[]{:S(2)}) copy-start(f32[16,128,256]{2,1,0:T(8,128)} %fusion.33) | copy-start | bytes 6291460
Sparse Core Ops, SparseCore 0:
  9.0 266.7 all-gather.1

commit v2 on v0

--- a/solution.py
+++ b/solution.py
@@ -8,12 +8,6 @@
 
 
 big_negative = -1e30
-
-
-def from_behind(block, axis, distance):
-    devices = range(lax.axis_size(axis))
-    route = [((i - distance) % len(devices), i) for i in devices]
-    return lax.ppermute(block, axis, route)
 
 
 def segment_ids(utt_ends, first_frame, frames):
@@ -61,17 +55,47 @@
         jnp.zeros((frames, HQ), jnp.float32),
         jnp.zeros((frames, HQ, HD), jnp.float32),
     )
+    gathered_weight = lax.all_gather(out_weight, "dp", axis=0, tiled=True)
     kv_block = jnp.concatenate([key_rows, value_rows], axis=0)
-    carry_state = absorb(initial, kv_block, cycle_place)
-    travelling = kv_block
-    for hop_index in range(1, cycle_size):
-        travelling = from_behind(travelling, "ctx", 1)
-        carry_state = absorb(carry_state, travelling, (cycle_place - hop_index) % cycle_size)
+    plane_size = cycle_size // 2
+    plane = cycle_place // plane_size
+    spot = cycle_place % plane_size
+    half = frames // 2
+
+    def in_plane(block, step):
+        route = [
+            (i, (i // plane_size) * plane_size + (i % plane_size + step) % plane_size)
+            for i in range(cycle_size)
+        ]
+        return lax.ppermute(block, "ctx", route)
+
+    def around(block, source_plane):
+        ahead = in_plane(block, 1)
+        behind = in_plane(block, -1)
+        ahead_two = in_plane(ahead[:, :half], 1)
+        behind_two = in_plane(behind[:, half:], -1)
+        far = jnp.concatenate([ahead_two, behind_two], axis=1)
+        base = source_plane * plane_size
+        return [
+            (ahead, base + (spot - 1) % plane_size),
+            (behind, base + (spot + 1) % plane_size),
+            (far, base + (spot + 2) % plane_size),
+        ]
+
+    partner = lax.ppermute(
+        kv_block, "ctx", [(i, (i + plane_size) % cycle_size) for i in range(cycle_size)]
+    )
+    arrivals = [(kv_block, cycle_place)] + around(kv_block, plane)
+    arrivals += [(partner, (cycle_place + plane_size) % cycle_size)]
+    arrivals += around(partner, 1 - plane)
+    carry_state = initial
+    for block, source in arrivals:
+        carry_state = absorb(carry_state, block, source)
     max_final, denom_final, numerator = carry_state
     attn_rows = (numerator / denom_final[:, :, None]).reshape(frames, HQ * HD).astype(jnp.bfloat16)
     summed = jnp.dot(
         attn_rows,
-        lax.all_gather(out_weight, "dp", axis=0, tiled=True),
+        gathered_weight,
         preferred_element_type=jnp.float32,
     )
     return summed.astype(jnp.bfloat16)[None]

time: 433 us -> 230 us (0.53)
  waiting for transfers between devices: 350 us -> 137 us
  starting transfers between devices: 1.66 us -> 14.4 us
    ppermute x7 -> x9, waiting for transfers between devices: 323 us -> 137 us  [the longest x8 93.9 us: in_plane(): return lax.ppermute(block, 'ctx', route)]
    all_gather x1, waiting for transfers between devices: 25.9 us -> 0.02 us  [shards(): gathered_weight = lax.all_gather(out_weight, 'dp', axis=0, tiled=True)]
    ppermute x7 -> x9, starting transfers between devices: 1.66 us -> 14.3 us  [the longest x8 13.8 us: in_plane(): return lax.ppermute(block, 'ctx', route)]
  transfers between devices with their start and end apart: 8 -> 10, of which waited for: 8 -> 6; matrix products, arithmetic and copies ran while one was open for 11% -> 21% of each run, Pallas kernels for 0% -> 0%
where the time goes in v2:
time: 230 us; the launch traced here: 227 us
  waiting for transfers between devices  137 us (60%)
  matrix products  36 us (16%)
  starting transfers between devices  14.4 us (6%)
  between operations  14 us (6%)
  local copies, waits for them, and re-layouts  13.8 us (6%)
  other arithmetic  12 us (5%)
    ppermute x8, waiting for transfers between devices, in_plane(): return lax.ppermute(block, 'ctx', route)  93.9 us
    ppermute x1, waiting for transfers between devices, shards(): lax.ppermute(kv_block, 'ctx', [(i, (i + plane_size) % cycle_size) for i i...  42.7 us
    dot_general x8, matrix products, attend(): jnp.einsum('qhk,khd->qhd', weights.astype(jnp.bfloat16), value_heads, pre...  16.2 us
    ppermute x8, starting transfers between devices, in_plane(): return lax.ppermute(block, 'ctx', route)  13.8 us
    dot_general x1, matrix products, shards(): jnp.dot(attn_rows, gathered_weight, preferred_element_type=jnp.float32)  11.5 us
    reduce_sum x8, other arithmetic, attend(): denom_new = denom_old * rescale + jnp.sum(weights, axis=2)  8.39 us
    dot_general x8, matrix products, attend(): jnp.einsum('qhd,khd->qhk', query_heads, key_heads, preferred_element_type...  8.24 us
    unnamed x51, local copies, waits for them, and re-layouts  6.23 us
  transfers between devices with their start and end apart: 10, of which 6 were waited for; matrix products, arithmetic and copies ran while one was open for 21% of the time, Pallas kernels for 0%

profile of v2, /device:TPU:102, one launch (start us, length us, event | category | flops | bytes accessed | tf_op | source)
XLA Modules:
  0.0 227.4 jit_solution(8332168899340255902)
XLA Ops:
  7.3 1.5 copy.100
  8.8 1.9 copy.62
  10.7 1.5 pad_maximum_fusion
  12.2 1.6 collective-permute-start
  13.7 1.7 collective-permute-start.1
  16.1 1.4 copy.102
  19.6 41.5 %collective-permute-done = bf16[2,256,2048]{1,2,0:T(8,128)(2,1)S(1)} collective-permute-done((bf16[2,256,2048]{1,2,0:T(8,128)(2,1)}, bf16[2,256,2048]{1,2,0:T(8,128)(2,1)S(1)}, u32[]{:S(2)}, u32[]{:S(2)}) %collective-permute-start) | collective-permute-done | bytes 2097184 | tf_op jit(solution)/shard_map/ppermute | solution.py:70
  61.5 1.3 slice.77
  62.8 3.0 %collective-permute-start.3 = (bf16[2,128,2048]{1,2,0:T(8,128)(2,1)S(1)}, bf16[2,128,2048]{1,2,0:T(8,128)(2,1)S(1)}, u32[]{:S(2)}, u32[]{:S(2)}) collective-permute-start(bf16[2,128,2048]{1,2,0:T(8,128)(2,1)S(1)} %slice.77), channel_id=1, source_target_pairs={{0,3},{1,0},{2,1},{3,2},{4,7},{5,4},{6,5},{7,6},{8,11},{9,8},{10,9... | collective-permute-start | bytes 3145736 | tf_op jit(solution)/shard_map/ppermute | solution.py:70
  65.8 42.7 %collective-permute-done.4 = bf16[2,256,2048]{1,2,0:T(8,128)(2,1)} collective-permute-done((bf16[2,256,2048]{1,2,0:T(8,128)(2,1)}, bf16[2,256,2048]{1,2,0:T(8,128)(2,1)}, u32[]{:S(2)}, u32[]{:S(2)}) %collective-permute-start.4) | collective-permute-done | bytes 2097184 | tf_op jit(solution)/shard_map/ppermute | solution.py:85
  108.5 1.7 fusion.140
  110.2 1.7 fusion.138
  112.1 1.0 fusion.5
  113.1 3.4 %collective-permute-start.6 = (bf16[2,256,2048]{1,2,0:T(8,128)(2,1)}, bf16[2,256,2048]{1,2,0:T(8,128)(2,1)S(1)}, u32[]{:S(2)}, u32[]{:S(2)}) collective-permute-start(bf16[2,256,2048]{1,2,0:T(8,128)(2,1)} %collective-permute-done.4), channel_id=1, source_target_pairs={{0,3},{1,0},{2,1},{3,2},{4,7},{5,4},{6,5},{7,6},{8,11},{9,8},{10,9... | collective-permute-start | bytes 6291464 | tf_op jit(solution)/shard_map/ppermute | solution.py:70
  117.6 1.0 fusion.2
  119.2 1.0 fusion.4
  120.3 34.1 %collective-permute-done.5 = bf16[2,256,2048]{1,2,0:T(8,128)(2,1)S(1)} collective-permute-done((bf16[2,256,2048]{1,2,0:T(8,128)(2,1)}, bf16[2,256,2048]{1,2,0:T(8,128)(2,1)S(1)}, u32[]{:S(2)}, u32[]{:S(2)}) %collective-permute-start.5) | collective-permute-done | bytes 2097184 | tf_op jit(solution)/shard_map/ppermute | solution.py:70
  154.5 4.2 %collective-permute-done.6 = bf16[2,256,2048]{1,2,0:T(8,128)(2,1)S(1)} collective-permute-done((bf16[2,256,2048]{1,2,0:T(8,128)(2,1)}, bf16[2,256,2048]{1,2,0:T(8,128)(2,1)S(1)}, u32[]{:S(2)}, u32[]{:S(2)}) %collective-permute-start.6) | collective-permute-done | bytes 2097184 | tf_op jit(solution)/shard_map/ppermute | solution.py:70
  158.8 3.7 %collective-permute-start.8 = (bf16[2,128,2048]{1,2,0:T(8,128)(2,1)S(1)}, bf16[2,128,2048]{1,2,0:T(8,128)(2,1)S(1)}, u32[]{:S(2)}, u32[]{:S(2)}) collective-permute-start(bf16[2,128,2048]{1,2,0:T(8,128)(2,1)S(1)} %slice.87), channel_id=1, source_target_pairs={{0,3},{1,0},{2,1},{3,2},{4,7},{5,4},{6,5},{7,6},{8,11},{9,8},{10,9... | collective-permute-start | bytes 3145736 | tf_op jit(solution)/shard_map/ppermute | solution.py:70
  163.9 1.0 fusion.7
  164.9 10.3 %collective-permute-done.7 = bf16[2,128,2048]{1,2,0:T(8,128)(2,1)S(1)} collective-permute-done((bf16[2,128,2048]{1,2,0:T(8,128)(2,1)S(1)}, bf16[2,128,2048]{1,2,0:T(8,128)(2,1)S(1)}, u32[]{:S(2)}, u32[]{:S(2)}) %collective-permute-start.7) | collective-permute-done | bytes 1048608 | tf_op jit(solution)/shard_map/ppermute | solution.py:70
  175.4 3.8 %collective-permute-done.8 = bf16[2,128,2048]{1,2,0:T(8,128)(2,1)S(1)} collective-permute-done((bf16[2,128,2048]{1,2,0:T(8,128)(2,1)S(1)}, bf16[2,128,2048]{1,2,0:T(8,128)(2,1)S(1)}, u32[]{:S(2)}, u32[]{:S(2)}) %collective-permute-start.8) | collective-permute-done | bytes 1048608 | tf_op jit(solution)/shard_map/ppermute | solution.py:70
  188.4 1.2 fusion.23
  190.4 2.5 %fusion.39 = f32[16,256,128]{1,2,0:T(8,128)} fusion(bf16[256,16,128]{0,2,1:T(8,128)(2,1)S(1)} %bitcast.197, f32[16,256,256]{2,1,0:T(8,128)S(1)} %get-tuple-element.67, f32[256,16]{0,1:T(8,128)S(1)} %get-tuple-element.43, pred[256,256]{0,1:T(8,128)(4,1)S(1)} %copy-done.6), kind=kOutput, calls=%fused_computation.49 | convolution fusion | flops 273678336 | bytes 7421952 | tf_op jit(solution)/shard_map/qhk,khd->qhd/dot_general | solution.py:32
  192.9 2.5 %fusion.37 = f32[16,128,256]{2,1,0:T(8,128)} fusion(bf16[256,16,128]{0,2,1:T(8,128)(2,1)S(1)} %bitcast.203, f32[16,256,256]{2,1,0:T(8,128)S(1)} %get-tuple-element.65, f32[256,16]{0,1:T(8,128)S(1)} %get-tuple-element.27, pred[256,256]{0,1:T(8,128)(4,1)S(1)} %copy-done.4), kind=kOutput, calls=%fused_computation.48 | convolution fusion | flops 273678336 | bytes 7421952 | tf_op jit(solution)/shard_map/qhk,khd->qhd/dot_general | solution.py:32
  195.4 1.2 fusion.35
  196.6 2.5 %fusion.33 = f32[16,128,256]{2,1,0:T(8,128)} fusion(bf16[256,16,128]{0,2,1:T(8,128)(2,1)S(1)} %bitcast.204, f32[16,256,256]{2,1,0:T(8,128)S(1)} %get-tuple-element.61, f32[256,16]{0,1:T(8,128)S(1)} %get-tuple-element.25, pred[256,256]{0,1:T(8,128)(4,1)S(1)} %get-tuple-element.46), kind=kOutput, calls=%fused_computation.46 | convolution fusion | flops 273678336 | bytes 7421952 | tf_op jit(solution)/shard_map/qhk,khd->qhd/dot_general | solution.py:32
  199.1 1.2 fusion.31
  200.3 2.5 %fusion.29 = f32[16,128,256]{2,1,0:T(8,128)} fusion(bf16[256,16,128]{0,2,1:T(8,128)(2,1)S(1)} %bitcast.206, f32[16,256,256]{2,1,0:T(8,128)S(1)} %get-tuple-element.57, f32[256,16]{0,1:T(8,128)S(1)} %get-tuple-element.23, pred[256,256]{0,1:T(8,128)(4,1)S(1)} %get-tuple-element.48), kind=kOutput, calls=%fused_computation.44 | convolution fusion | flops 273678336 | bytes 7421952 | tf_op jit(solution)/shard_map/qhk,khd->qhd/dot_general | solution.py:32
  202.9 1.2 fusion.25
  206.4 2.6 %fusion.42 = bf16[256,16,128]{0,2,1:T(8,128)(2,1)S(1)} fusion(f32[16,128,256]{2,1,0:T(8,128)S(1)} %fusion.25, f32[16,128,256]{2,1,0:T(8,128)S(1)} %copy-done.22, f32[16,128,256]{2,1,0:T(8,128)S(1)} %fusion.31, f32[16,128,256]{2,1,0:T(8,128)S(1)} %copy-done.21, f32[16,128,256]{2,1,0:T(8,128)S(1)} %fusion.35, f32[16,128,256]{2,1,0:T(8,128)S(1)} %copy-done.20, ...), kind=kOutput, calls=%fused_computation.53 | convolution fusion | flops 282591232 | bytes 21200896 | tf_op jit(solution)/shard_map/qhk,khd->qhd/dot_general | solution.py:32
  209.1 11.5 %fusion = bf16[1,256,4096]{2,1,0:T(8,128)(2,1)} fusion(bf16[256,2048]{0,1:T(8,128)(2,1)S(1)} %bitcast.198, bf16[2048,4096]{1,0:T(8,128)(2,1)} %all-gather.2.cloned.1.call-done), kind=kOutput, calls=%fused_computation.1 | convolution fusion | flops 4296015872 | bytes 19922944 | tf_op jit(solution)/shard_map/dot_general | solution.py:96
  (89 shorter events, 19.4 us)
Async XLA Ops:
  6.5 202.5 %all-gather.2.cloned.1.call-start = ((), (), s32[]{:S(2)}) async-start(), calls=%async_computation | async-start | bytes 17825792 | tf_op jit(solution)/shard_map/all_gather | solution.py:58
  7.3 8.7 %copy-start.18 = (s32[1,8]{1,0:T(1,128)S(1)}, s32[1,8]{1,0:T(1,128)}, u32[]{:S(2)}) copy-start(s32[1,8]{1,0:T(1,128)} %param.8) | copy-start | bytes 100
  8.8 1.9 copy-start.1
  8.8 8.8 %copy-start = (bf16[1,256,2048]{2,1,0:T(8,128)(2,1)S(1)}, bf16[1,256,2048]{2,1,0:T(8,128)(2,1)}, u32[]{:S(2)}) copy-start(bf16[1,256,2048]{2,1,0:T(8,128)(2,1)} %param.6) | copy-start | bytes 3145732
  12.2 48.9 %collective-permute-start = (bf16[2,256,2048]{1,2,0:T(8,128)(2,1)}, bf16[2,256,2048]{1,2,0:T(8,128)(2,1)S(1)}, u32[]{:S(2)}, u32[]{:S(2)}) collective-permute-start(bf16[2,256,2048]{1,2,0:T(8,128)(2,1)} %pad_maximum_fusion), channel_id=1, source_target_pairs={{0,1},{1,2},{2,3},{3,0},{4,5},{5,6},{6,7},{7,4},{8,9},{9,10},{10,1... | collective-permute-start | bytes 6291464 | tf_op jit(solution)/shard_map/ppermute | solution.py:70
  13.7 47.7 %collective-permute-start.1 = (bf16[2,256,2048]{1,2,0:T(8,128)(2,1)}, bf16[2,256,2048]{1,2,0:T(8,128)(2,1)}, u32[]{:S(2)}, u32[]{:S(2)}) collective-permute-start(bf16[2,256,2048]{1,2,0:T(8,128)(2,1)} %pad_maximum_fusion), channel_id=1, source_target_pairs={{0,3},{1,0},{2,1},{3,2},{4,7},{5,4},{6,5},{7,6},{8,11},{9,8},{10,9... | collective-permute-start | bytes 6291464 | tf_op jit(solution)/shard_map/ppermute | solution.py:70
  15.4 93.1 %collective-permute-start.4 = (bf16[2,256,2048]{1,2,0:T(8,128)(2,1)}, bf16[2,256,2048]{1,2,0:T(8,128)(2,1)}, u32[]{:S(2)}, u32[]{:S(2)}) collective-permute-start(bf16[2,256,2048]{1,2,0:T(8,128)(2,1)} %pad_maximum_fusion), channel_id=1, source_target_pairs={{0,4},{1,5},{2,6},{3,7},{4,0},{5,1},{6,2},{7,3},{8,12},{9,13},{10,... | collective-permute-start | bytes 6291464 | tf_op jit(solution)/shard_map/ppermute | solution.py:85
  18.5 42.6 %copy-start.5 = (pred[256,256]{0,1:T(8,128)(4,1)}, pred[256,256]{0,1:T(8,128)(4,1)S(1)}, u32[]{:S(2)}) copy-start(pred[256,256]{0,1:T(8,128)(4,1)S(1)} %get-tuple-element.44) | copy-start | bytes 196612
  18.5 99.1 %copy-start.3 = (pred[256,256]{0,1:T(8,128)(4,1)}, pred[256,256]{0,1:T(8,128)(4,1)S(1)}, u32[]{:S(2)}) copy-start(pred[256,256]{0,1:T(8,128)(4,1)S(1)} %get-tuple-element.51) | copy-start | bytes 196612
  19.5 161.0 %copy-start.7 = (f32[256,16]{0,1:T(8,128)}, f32[256,16]{0,1:T(8,128)S(1)}, u32[]{:S(2)}) copy-start(f32[256,16]{0,1:T(8,128)S(1)} %get-tuple-element.66) | copy-start | bytes 49156
  61.1 57.5 %collective-permute-start.2 = (bf16[2,128,2048]{1,2,0:T(8,128)(2,1)S(1)}, bf16[2,128,2048]{1,2,0:T(8,128)(2,1)S(1)}, u32[]{:S(2)}, u32[]{:S(2)}) collective-permute-start(bf16[2,128,2048]{1,2,0:T(8,128)(2,1)S(1)} %slice.76), channel_id=1, source_target_pairs={{0,1},{1,2},{2,3},{3,0},{4,5},{5,6},{6,7},{7,4},{8,9},{9,10},{10,1... | collective-permute-start | bytes 3145736 | tf_op jit(solution)/shard_map/ppermute | solution.py:70
  62.8 56.0 %collective-permute-start.3 = (bf16[2,128,2048]{1,2,0:T(8,128)(2,1)S(1)}, bf16[2,128,2048]{1,2,0:T(8,128)(2,1)S(1)}, u32[]{:S(2)}, u32[]{:S(2)}) collective-permute-start(bf16[2,128,2048]{1,2,0:T(8,128)(2,1)S(1)} %slice.77), channel_id=1, source_target_pairs={{0,3},{1,0},{2,1},{3,2},{4,7},{5,4},{6,5},{7,6},{8,11},{9,8},{10,9... | collective-permute-start | bytes 3145736 | tf_op jit(solution)/shard_map/ppermute | solution.py:70
  108.5 45.9 %collective-permute-start.5 = (bf16[2,256,2048]{1,2,0:T(8,128)(2,1)}, bf16[2,256,2048]{1,2,0:T(8,128)(2,1)S(1)}, u32[]{:S(2)}, u32[]{:S(2)}) collective-permute-start(bf16[2,256,2048]{1,2,0:T(8,128)(2,1)} %collective-permute-done.4), channel_id=1, source_target_pairs={{0,1},{1,2},{2,3},{3,0},{4,5},{5,6},{6,7},{7,4},{8,9},{9,10},{10,1... | collective-permute-start | bytes 6291464 | tf_op jit(solution)/shard_map/ppermute | solution.py:70
  113.1 45.6 %collective-permute-start.6 = (bf16[2,256,2048]{1,2,0:T(8,128)(2,1)}, bf16[2,256,2048]{1,2,0:T(8,128)(2,1)S(1)}, u32[]{:S(2)}, u32[]{:S(2)}) collective-permute-start(bf16[2,256,2048]{1,2,0:T(8,128)(2,1)} %collective-permute-done.4), channel_id=1, source_target_pairs={{0,3},{1,0},{2,1},{3,2},{4,7},{5,4},{6,5},{7,6},{8,11},{9,8},{10,9... | collective-permute-start | bytes 6291464 | tf_op jit(solution)/shard_map/ppermute | solution.py:70
  154.5 20.7 %collective-permute-start.7 = (bf16[2,128,2048]{1,2,0:T(8,128)(2,1)S(1)}, bf16[2,128,2048]{1,2,0:T(8,128)(2,1)S(1)}, u32[]{:S(2)}, u32[]{:S(2)}) collective-permute-start(bf16[2,128,2048]{1,2,0:T(8,128)(2,1)S(1)} %slice.86), channel_id=1, source_target_pairs={{0,1},{1,2},{2,3},{3,0},{4,5},{5,6},{6,7},{7,4},{8,9},{9,10},{10,1... | collective-permute-start | bytes 3145736 | tf_op jit(solution)/shard_map/ppermute | solution.py:70
  158.8 20.3 %collective-permute-start.8 = (bf16[2,128,2048]{1,2,0:T(8,128)(2,1)S(1)}, bf16[2,128,2048]{1,2,0:T(8,128)(2,1)S(1)}, u32[]{:S(2)}, u32[]{:S(2)}) collective-permute-start(bf16[2,128,2048]{1,2,0:T(8,128)(2,1)S(1)} %slice.87), channel_id=1, source_target_pairs={{0,3},{1,0},{2,1},{3,2},{4,7},{5,4},{6,5},{7,6},{8,11},{9,8},{10,9... | collective-permute-start | bytes 3145736 | tf_op jit(solution)/shard_map/ppermute | solution.py:70
  179.5 1.7 copy-start.6
  179.5 2.7 %copy-start.4 = (pred[256,256]{0,1:T(8,128)(4,1)S(1)}, pred[256,256]{0,1:T(8,128)(4,1)}, u32[]{:S(2)}) copy-start(pred[256,256]{0,1:T(8,128)(4,1)} %copy-done.3) | copy-start | bytes 196612
  187.4 2.3 %copy-start.8 = (f32[256,16]{0,1:T(8,128)S(1)}, f32[256,16]{0,1:T(8,128)}, u32[]{:S(2)}) copy-start(f32[256,16]{0,1:T(8,128)} %copy-done.7) | copy-start | bytes 49156
  187.4 3.0 %copy-start.2 = (bf16[1,256,2048]{1,2,0:T(8,128)(2,1)S(1)}, bf16[1,256,2048]{1,2,0:T(8,128)(2,1)}, u32[]{:S(2)}) copy-start(bf16[1,256,2048]{1,2,0:T(8,128)(2,1)} %copy-done.1) | copy-start | bytes 3145732
  202.8 1.3 copy-start.10
  202.8 1.3 copy-start.11
  202.8 1.3 copy-start.12
  202.8 1.3 copy-start.13
  202.8 1.3 copy-start.14
  202.9 1.3 copy-start.15
  202.9 1.3 copy-start.16
  202.9 1.3 copy-start.17
  202.9 1.7 copy-start.19
  202.9 2.3 %copy-start.20 = (f32[16,128,256]{2,1,0:T(8,128)S(1)}, f32[16,128,256]{2,1,0:T(8,128)}, u32[]{:S(2)}) copy-start(f32[16,128,256]{2,1,0:T(8,128)} %fusion.37) | copy-start | bytes 6291460
  202.9 2.9 %copy-start.21 = (f32[16,128,256]{2,1,0:T(8,128)S(1)}, f32[16,128,256]{2,1,0:T(8,128)}, u32[]{:S(2)}) copy-start(f32[16,128,256]{2,1,0:T(8,128)} %fusion.33) | copy-start | bytes 6291460
  202.9 3.5 %copy-start.22 = (f32[16,128,256]{2,1,0:T(8,128)S(1)}, f32[16,128,256]{2,1,0:T(8,128)}, u32[]{:S(2)}) copy-start(f32[16,128,256]{2,1,0:T(8,128)} %fusion.29) | copy-start | bytes 6291460
  (1 other events, 1.3 us)
Sparse Core Ops, SparseCore 0:
  9.0 132.6 all-gather.1

commit v3 on v2

--- a/solution.py
+++ b/solution.py
@@ -90,7 +90,7 @@
     arrivals += around(partner, 1 - plane)
     carry_state = initial
     for block, source in arrivals:
-        carry_state = absorb(carry_state, block, source)
+        carry_state = lax.optimization_barrier(absorb(carry_state, block, source))
     max_final, denom_final, numerator = carry_state
     attn_rows = (numerator / denom_final[:, :, None]).reshape(frames, HQ * HD).astype(jnp.bfloat16)
     summed = jnp.dot(

time: 230 us -> 202 us (0.88)
  waiting for transfers between devices: 137 us -> 116 us
    ppermute x8, waiting for transfers between devices: 93.9 us -> 82.2 us  [in_plane(): return lax.ppermute(block, 'ctx', route)]
    ppermute x1, waiting for transfers between devices: 42.7 us -> 32.6 us  [shards(): lax.ppermute(kv_block, 'ctx', [(i, (i + plane_size) % cycle_size) for i i...]
    dot_general x8, matrix products: 16.2 us -> 13.9 us  [attend(): jnp.einsum('qhk,khd->qhd', weights.astype(jnp.bfloat16), value_heads, pre...]
    unnamed x51 -> x13, local copies, waits for them, and re-layouts: 6.23 us -> 5.42 us
  transfers between devices with their start and end apart: 10 -> 10, of which waited for: 6 -> 4; matrix products, arithmetic and copies ran while one was open for 21% -> 23% of each run, Pallas kernels for 0% -> 0%
where the time goes in v3:
time: 202 us; the launch traced here: 201 us
  waiting for transfers between devices  116 us (57%)
  matrix products  33.7 us (17%)
  starting transfers between devices  14.2 us (7%)
  between operations  14 us (7%)
  local copies, waits for them, and re-layouts  12.1 us (6%)
  other arithmetic  11.3 us (6%)
    ppermute x8, waiting for transfers between devices, in_plane(): return lax.ppermute(block, 'ctx', route)  82.2 us
    ppermute x1, waiting for transfers between devices, shards(): lax.ppermute(kv_block, 'ctx', [(i, (i + plane_size) % cycle_size) for i i...  32.6 us
    dot_general x8, matrix products, attend(): jnp.einsum('qhk,khd->qhd', weights.astype(jnp.bfloat16), value_heads, pre...  13.9 us
    ppermute x8, starting transfers between devices, in_plane(): return lax.ppermute(block, 'ctx', route)  13.6 us
    dot_general x1, matrix products, shards(): jnp.dot(attn_rows, gathered_weight, preferred_element_type=jnp.float32)  11.5 us
    dot_general x8, matrix products, attend(): jnp.einsum('qhd,khd->qhk', query_heads, key_heads, preferred_element_type...  8.35 us
    reduce_sum x8, other arithmetic, attend(): denom_new = denom_old * rescale + jnp.sum(weights, axis=2)  8.17 us
    unnamed x13, local copies, waits for them, and re-layouts  5.42 us
  transfers between devices with their start and end apart: 10, of which 4 were waited for; matrix products, arithmetic and copies ran while one was open for 23% of the time, Pallas kernels for 0%

profile of v3, /device:TPU:102, one launch (start us, length us, event | category | flops | bytes accessed | tf_op | source)
XLA Modules:
  0.0 200.8 jit_solution(14840272959294938018)
XLA Ops:
  7.3 1.5 copy.77
  8.8 1.6 copy.78
  10.3 1.5 pad_maximum_fusion
  11.8 1.6 collective-permute-start
  13.4 1.7 collective-permute-start.1
  15.8 1.5 copy.131
  20.6 2.1 %bitcast_add_fusion.7 = f32[256,16,128]{2,0,1:T(8,128)S(1)} fusion(f32[16,256,256]{2,1,0:T(8,128)S(1)} %get-tuple-element.98, f32[256,16]{0,1:T(8,128)S(1)} %broadcast_maximum_fusion, pred[256,256]{0,1:T(8,128)(4,1)S(1)} %get-tuple-element.96, bf16[256,16,128]{2,1,0:T(8,128)(2,1)S(1)} %bitcast.183, f32[256,16]{0,1:T(8,128)S(1)} %get-tuple-element.87), kind=kOutput, calls=%fused_computation.58 | convolution fusion | flops 274202624 | bytes 7438336 | tf_op jit(solution)/shard_map/qhk,khd->qhd/dot_general | solution.py:32
  22.7 38.1 %collective-permute-done = bf16[2,256,2048]{1,2,0:T(8,128)(2,1)} collective-permute-done((bf16[2,256,2048]{1,2,0:T(8,128)(2,1)}, bf16[2,256,2048]{1,2,0:T(8,128)(2,1)}, u32[]{:S(2)}, u32[]{:S(2)}) %collective-permute-start) | collective-permute-done | bytes 2097184 | tf_op jit(solution)/shard_map/ppermute | solution.py:70
  60.8 1.7 fusion.146
  62.5 1.0 fusion.2
  64.6 1.7 bitcast_add_fusion.6
  66.3 1.3 slice.76
  68.3 1.0 fusion.3
  70.4 1.7 bitcast_add_fusion.5
  72.2 3.1 %collective-permute-start.3 = (bf16[2,128,2048]{1,2,0:T(8,128)(2,1)S(1)}, bf16[2,128,2048]{1,2,0:T(8,128)(2,1)S(1)}, u32[]{:S(2)}, u32[]{:S(2)}) collective-permute-start(bf16[2,128,2048]{1,2,0:T(8,128)(2,1)S(1)} %slice.77), channel_id=1, source_target_pairs={{0,3},{1,0},{2,1},{3,2},{4,7},{5,4},{6,5},{7,6},{8,11},{9,8},{10,9... | collective-permute-start | bytes 3145736 | tf_op jit(solution)/shard_map/ppermute | solution.py:70
  75.2 32.6 %collective-permute-done.4 = bf16[2,256,2048]{1,2,0:T(8,128)(2,1)} collective-permute-done((bf16[2,256,2048]{1,2,0:T(8,128)(2,1)}, bf16[2,256,2048]{1,2,0:T(8,128)(2,1)}, u32[]{:S(2)}, u32[]{:S(2)}) %collective-permute-start.4) | collective-permute-done | bytes 2097184 | tf_op jit(solution)/shard_map/ppermute | solution.py:85
  107.9 3.2 %collective-permute-start.6 = (bf16[2,256,2048]{1,2,0:T(8,128)(2,1)}, bf16[2,256,2048]{1,2,0:T(8,128)(2,1)S(1)}, u32[]{:S(2)}, u32[]{:S(2)}) collective-permute-start(bf16[2,256,2048]{1,2,0:T(8,128)(2,1)} %collective-permute-done.4), channel_id=1, source_target_pairs={{0,3},{1,0},{2,1},{3,2},{4,7},{5,4},{6,5},{7,6},{8,11},{9,8},{10,9... | collective-permute-start | bytes 6291464 | tf_op jit(solution)/shard_map/ppermute | solution.py:70
  111.1 1.7 fusion.143
  112.8 1.0 fusion.5
  114.4 1.0 fusion.4
  116.6 1.7 bitcast_add_fusion.4
  119.3 1.7 bitcast_add_fusion.3
  121.0 31.0 %collective-permute-done.5 = bf16[2,256,2048]{1,2,0:T(8,128)(2,1)S(1)} collective-permute-done((bf16[2,256,2048]{1,2,0:T(8,128)(2,1)}, bf16[2,256,2048]{1,2,0:T(8,128)(2,1)S(1)}, u32[]{:S(2)}, u32[]{:S(2)}) %collective-permute-start.5) | collective-permute-done | bytes 2097184 | tf_op jit(solution)/shard_map/ppermute | solution.py:70
  152.2 1.0 fusion.6
  154.3 1.7 bitcast_add_fusion.2
  156.2 3.5 %collective-permute-start.8 = (bf16[2,128,2048]{1,2,0:T(8,128)(2,1)S(1)}, bf16[2,128,2048]{1,2,0:T(8,128)(2,1)S(1)}, u32[]{:S(2)}, u32[]{:S(2)}) collective-permute-start(bf16[2,128,2048]{1,2,0:T(8,128)(2,1)S(1)} %slice.87), channel_id=1, source_target_pairs={{0,3},{1,0},{2,1},{3,2},{4,7},{5,4},{6,5},{7,6},{8,11},{9,8},{10,9... | collective-permute-start | bytes 3145736 | tf_op jit(solution)/shard_map/ppermute | solution.py:70
  159.9 1.0 fusion.7
  162.0 1.7 bitcast_add_fusion.1
  163.7 13.1 %collective-permute-done.7 = bf16[2,128,2048]{1,2,0:T(8,128)(2,1)S(1)} collective-permute-done((bf16[2,128,2048]{1,2,0:T(8,128)(2,1)S(1)}, bf16[2,128,2048]{1,2,0:T(8,128)(2,1)S(1)}, u32[]{:S(2)}, u32[]{:S(2)}) %collective-permute-start.7) | collective-permute-done | bytes 1048608 | tf_op jit(solution)/shard_map/ppermute | solution.py:70
  177.4 1.0 fusion.8
  179.5 1.7 bitcast_add_fusion
  182.5 11.5 %fusion = bf16[1,256,4096]{2,1,0:T(8,128)(2,1)} fusion(bf16[256,2048]{0,1:T(8,128)(2,1)S(1)} %bitcast.172, bf16[2048,4096]{1,0:T(8,128)(2,1)} %all-gather.2.cloned.1.call-done), kind=kOutput, calls=%fused_computation.1 | convolution fusion | flops 4296015872 | bytes 19922944 | tf_op jit(solution)/shard_map/dot_general | solution.py:96
  (66 shorter events, 15.5 us)
Async XLA Ops:
  6.5 175.9 %all-gather.2.cloned.1.call-start = ((), (), s32[]{:S(2)}) async-start(), calls=%async_computation | async-start | bytes 17825792 | tf_op jit(solution)/shard_map/all_gather | solution.py:58
  7.3 8.4 %copy-start.2 = (s32[1,8]{1,0:T(1,128)S(1)}, s32[1,8]{1,0:T(1,128)}, u32[]{:S(2)}) copy-start(s32[1,8]{1,0:T(1,128)} %param.8) | copy-start | bytes 100
  8.8 8.6 %copy-start = (bf16[1,256,2048]{2,1,0:T(8,128)(2,1)S(1)}, bf16[1,256,2048]{2,1,0:T(8,128)(2,1)}, u32[]{:S(2)}) copy-start(bf16[1,256,2048]{2,1,0:T(8,128)(2,1)} %param.6) | copy-start | bytes 3145732
  11.8 49.0 %collective-permute-start = (bf16[2,256,2048]{1,2,0:T(8,128)(2,1)}, bf16[2,256,2048]{1,2,0:T(8,128)(2,1)}, u32[]{:S(2)}, u32[]{:S(2)}) collective-permute-start(bf16[2,256,2048]{1,2,0:T(8,128)(2,1)} %pad_maximum_fusion), channel_id=1, source_target_pairs={{0,1},{1,2},{2,3},{3,0},{4,5},{5,6},{6,7},{7,4},{8,9},{9,10},{10,1... | collective-permute-start | bytes 6291464 | tf_op jit(solution)/shard_map/ppermute | solution.py:70
  13.4 54.7 %collective-permute-start.1 = (bf16[2,256,2048]{1,2,0:T(8,128)(2,1)}, bf16[2,256,2048]{1,2,0:T(8,128)(2,1)S(1)}, u32[]{:S(2)}, u32[]{:S(2)}) collective-permute-start(bf16[2,256,2048]{1,2,0:T(8,128)(2,1)} %pad_maximum_fusion), channel_id=1, source_target_pairs={{0,3},{1,0},{2,1},{3,2},{4,7},{5,4},{6,5},{7,6},{8,11},{9,8},{10,9... | collective-permute-start | bytes 6291464 | tf_op jit(solution)/shard_map/ppermute | solution.py:70
  15.1 92.8 %collective-permute-start.4 = (bf16[2,256,2048]{1,2,0:T(8,128)(2,1)}, bf16[2,256,2048]{1,2,0:T(8,128)(2,1)}, u32[]{:S(2)}, u32[]{:S(2)}) collective-permute-start(bf16[2,256,2048]{1,2,0:T(8,128)(2,1)} %pad_maximum_fusion), channel_id=1, source_target_pairs={{0,4},{1,5},{2,6},{3,7},{4,0},{5,1},{6,2},{7,3},{8,12},{9,13},{10,... | collective-permute-start | bytes 6291464 | tf_op jit(solution)/shard_map/ppermute | solution.py:85
  15.8 1.8 copy-start.1
  67.6 46.2 %collective-permute-start.2 = (bf16[2,128,2048]{1,2,0:T(8,128)(2,1)S(1)}, bf16[2,128,2048]{1,2,0:T(8,128)(2,1)S(1)}, u32[]{:S(2)}, u32[]{:S(2)}) collective-permute-start(bf16[2,128,2048]{1,2,0:T(8,128)(2,1)S(1)} %slice.76), channel_id=1, source_target_pairs={{0,1},{1,2},{2,3},{3,0},{4,5},{5,6},{6,7},{7,4},{8,9},{9,10},{10,1... | collective-permute-start | bytes 3145736 | tf_op jit(solution)/shard_map/ppermute | solution.py:70
  72.2 41.9 %collective-permute-start.3 = (bf16[2,128,2048]{1,2,0:T(8,128)(2,1)S(1)}, bf16[2,128,2048]{1,2,0:T(8,128)(2,1)S(1)}, u32[]{:S(2)}, u32[]{:S(2)}) collective-permute-start(bf16[2,128,2048]{1,2,0:T(8,128)(2,1)S(1)} %slice.77), channel_id=1, source_target_pairs={{0,3},{1,0},{2,1},{3,2},{4,7},{5,4},{6,5},{7,6},{8,11},{9,8},{10,9... | collective-permute-start | bytes 3145736 | tf_op jit(solution)/shard_map/ppermute | solution.py:70
  107.9 44.2 %collective-permute-start.5 = (bf16[2,256,2048]{1,2,0:T(8,128)(2,1)}, bf16[2,256,2048]{1,2,0:T(8,128)(2,1)S(1)}, u32[]{:S(2)}, u32[]{:S(2)}) collective-permute-start(bf16[2,256,2048]{1,2,0:T(8,128)(2,1)} %collective-permute-done.4), channel_id=1, source_target_pairs={{0,1},{1,2},{2,3},{3,0},{4,5},{5,6},{6,7},{7,4},{8,9},{9,10},{10,1... | collective-permute-start | bytes 6291464 | tf_op jit(solution)/shard_map/ppermute | solution.py:70
  107.9 48.3 %collective-permute-start.6 = (bf16[2,256,2048]{1,2,0:T(8,128)(2,1)}, bf16[2,256,2048]{1,2,0:T(8,128)(2,1)S(1)}, u32[]{:S(2)}, u32[]{:S(2)}) collective-permute-start(bf16[2,256,2048]{1,2,0:T(8,128)(2,1)} %collective-permute-done.4), channel_id=1, source_target_pairs={{0,3},{1,0},{2,1},{3,2},{4,7},{5,4},{6,5},{7,6},{8,11},{9,8},{10,9... | collective-permute-start | bytes 6291464 | tf_op jit(solution)/shard_map/ppermute | solution.py:70
  156.1 20.7 %collective-permute-start.7 = (bf16[2,128,2048]{1,2,0:T(8,128)(2,1)S(1)}, bf16[2,128,2048]{1,2,0:T(8,128)(2,1)S(1)}, u32[]{:S(2)}, u32[]{:S(2)}) collective-permute-start(bf16[2,128,2048]{1,2,0:T(8,128)(2,1)S(1)} %slice.86), channel_id=1, source_target_pairs={{0,1},{1,2},{2,3},{3,0},{4,5},{5,6},{6,7},{7,4},{8,9},{9,10},{10,1... | collective-permute-start | bytes 3145736 | tf_op jit(solution)/shard_map/ppermute | solution.py:70
  156.2 20.7 %collective-permute-start.8 = (bf16[2,128,2048]{1,2,0:T(8,128)(2,1)S(1)}, bf16[2,128,2048]{1,2,0:T(8,128)(2,1)S(1)}, u32[]{:S(2)}, u32[]{:S(2)}) collective-permute-start(bf16[2,128,2048]{1,2,0:T(8,128)(2,1)S(1)} %slice.87), channel_id=1, source_target_pairs={{0,3},{1,0},{2,1},{3,2},{4,7},{5,4},{6,5},{7,6},{8,11},{9,8},{10,9... | collective-permute-start | bytes 3145736 | tf_op jit(solution)/shard_map/ppermute | solution.py:70
Sparse Core Ops, SparseCore 0:
  9.0 132.2 all-gather.1
